TPU v7x, 32 devices: a whole 2x2x4 slice. The times are simulated.
32 devices in a mesh: gx: 8 (over z, x), gy: 4 (over y, core).
Axes of the slice: x: 2, y: 2, z: 4, core: 2. Of those that a mesh axis runs over, the one named last changes fastest.
Arguments:
- prior_basis: float32 [128, 128, 128], P('gx', 'gy'), may hold values from -6 to 6
- cond_x: float32 [128, 128], P('gx', 'gy'), may hold values from 0.5 to 5
- cond_y: float32 [128, 128], P('gx', 'gy'), may hold values from 0.5 to 5
- capacitance: float32 [128, 128], P('gx', 'gy'), may hold values from 0.05 to 1
- pad_mask: int32 [128, 128], P('gx', 'gy'), may hold values 0 or 1
- port_nodes: int32 [128], replicated, may hold values from 0 to 16383
Outputs:
- new_basis: float32 [128, 128, 128], P('gx', 'gy')
- reduced_g: float32 [128, 128], replicated
- reduced_c: float32 [128, 128], replicated
Inputs may be any that keep to these rules, and one draw needn't show every extreme that they name: `port_nodes`: a row-major node index into the grid of 128 x 128 nodes.
All inputs are finite; a program needn't handle non-finite values. No bound on the sum of `pad_mask` on one device may be relied on, other than what follows from the above.
Results may differ from a plain program's by a relative error of at most 0.0003.
Values sent between devices are 32-bit elements; how exact they have to be, the bound alone decides.
No kernel may reach another device: no remote copies, remote signals or barrier semaphores. Data moves between devices by JAX's collectives and lax.ppermute only.
A program may use at most 64 MiB of HBM per device.

v0:
```python
import jax
import jax.numpy as jnp
from jax import lax
from jax.sharding import PartitionSpec as P

SWEEPS = 4
shift_point = 0.5
supply_conductance = 4.0
port_current = 8.0
highest = lax.Precision.HIGHEST


def shifted(shard, axis, by):
    devices = lax.axis_size(axis)
    pairs = [(i, i + by) for i in range(devices) if 0 <= i + by < devices]
    return lax.ppermute(shard, axis, pairs)


def padded(cells, sides, width):
    for axis, dim in sides:
        count = lax.axis_size(axis)
        ends = count - 1
        head = lax.slice_in_dim(cells, 0, width, axis=dim)
        tail = lax.slice_in_dim(cells, cells.shape[dim] - width, cells.shape[dim], axis=dim)
        cells = jnp.concatenate(
            [
                lax.ppermute(tail, axis, [(i, (i + 1) % count) for i in range(ends)]),
                cells,
                lax.ppermute(head, axis, [((i + 1) % count, i) for i in range(ends)]),
            ],
            axis=dim,
        )
    return cells


def neighbors(ext, links):
    cx, cy, cx_up, cy_left = links
    total = cx[:, :, None] * ext[2:, 1:-1] + cx_up[:, :, None] * ext[:-2, 1:-1]
    return total + cy[:, :, None] * ext[1:-1, 2:] + cy_left[:, :, None] * ext[1:-1, :-2]


def local_inner(left, right):
    a = left.reshape(-1, left.shape[-1])
    b = right.reshape(-1, right.shape[-1])
    return jnp.einsum("cp,cq->pq", a, b, precision=highest, preferred_element_type=jnp.float32)


def per_device(prior_basis, cond_x, cond_y, capacitance, pad_mask, port_nodes):
    rows_dev, cols_dev = cond_x.shape
    width = port_nodes.shape[0]
    count_x = lax.axis_size("gx")
    count_y = lax.axis_size("gy")
    total_rows = rows_dev * count_x
    total_cols = cols_dev * count_y
    nodes = total_rows * total_cols
    row_start = lax.axis_index("gx") * rows_dev
    col_start = lax.axis_index("gy") * cols_dev
    global_rows = row_start + jnp.arange(rows_dev, dtype=jnp.int32)[:, None]
    global_cols = col_start + jnp.arange(cols_dev, dtype=jnp.int32)[None, :]
    cx = jnp.where(global_rows < total_rows - 1, cond_x, jnp.float32(0.0))
    cy = jnp.where(global_cols < total_cols - 1, cond_y, jnp.float32(0.0))
    above = shifted(cx[-1:, :], "gx", 1)
    beside = shifted(cy[:, -1:], "gy", 1)
    cx_up = jnp.concatenate([above, cx[:-1]], axis=0)
    cy_left = jnp.concatenate([beside, cy[:, :-1]], axis=1)
    links = (cx, cy, cx_up, cy_left)
    diag_g = cx + cx_up + cy + cy_left + supply_conductance * pad_mask.astype(jnp.float32)
    diag = (diag_g + shift_point * capacitance)[:, :, None]
    node_ids = global_rows * total_cols + global_cols
    onehot = (node_ids[:, :, None] == port_nodes[None, None, :]).astype(jnp.float32)
    rhs = capacitance[:, :, None] * prior_basis + port_current * onehot

    def sweep(step, current):
        ext = padded(current, (("gx", 0), ("gy", 1)), 1)
        return (rhs + neighbors(ext, links)) / diag

    field = lax.fori_loop(0, SWEEPS, sweep, rhs / diag)
    proj = lax.psum(local_inner(prior_basis, field), ("gx", "gy")) / nodes
    cand = field - jnp.einsum("xyk,kp->xyp", prior_basis, proj, precision=highest)
    gram = lax.psum(local_inner(cand, cand), ("gx", "gy")) / nodes
    lower = jnp.linalg.cholesky(gram)
    flat = cand.reshape(-1, width)
    basis_flat = lax.linalg.triangular_solve(
        lower, flat, left_side=False, lower=True, transpose_a=True
    )
    new_basis = basis_flat.reshape(rows_dev, cols_dev, width)
    ext = padded(new_basis, (("gx", 0), ("gy", 1)), 1)
    g_image = diag_g[:, :, None] * new_basis - neighbors(ext, links)
    g_raw, c_raw = lax.psum(
        (
            local_inner(new_basis, g_image),
            local_inner(new_basis, capacitance[:, :, None] * new_basis),
        ),
        ("gx", "gy"),
    )
    reduced_g = g_raw / nodes
    reduced_c = c_raw / nodes
    return (new_basis, reduced_g, reduced_c)


def solution(mesh):
    placed = (P("gx", "gy", None), P("gx", "gy"), P("gx", "gy"), P("gx", "gy"), P("gx", "gy"), P())
    return jax.shard_map(
        per_device,
        mesh=mesh,
        in_specs=placed,
        out_specs=(P("gx", "gy", None), P(), P()),
        check_vma=False,
    )
```

profile of v0, /device:TPU:0, one launch (start us, length us, event | category | flops | bytes accessed | tf_op | source)
XLA Modules:
  0.0 506.1 jit_solution(9967310550308028480)
XLA Ops:
  7.9 2.5 collective-permute-start.5
  10.5 4.2 collective-permute-start.4
  14.9 1.2 collective-permute-done.4
  16.8 1.2 broadcast_divide_fusion
  18.0 68.9 %while.10 = (s32[]{:T(128)}, f32[16,32,128]{2,1,0:T(8,128)S(1)}, f32[16,32]{1,0:T(8,128)S(1)}, f32[16,32]{1,0:T(8,128)S(1)}, f32[16,32]{1,0:T(8,128)S(1)}, /*ind...) while((s32[]{:T(128)}, f32[16,32,128]{2,1,0:T(8,128)S(1)}, ...), condition=%wide.region_1.2_spmd, body=%wide.region_0.1_spmd.sunk | while | flops 851970 | bytes 2564349 | solution.py:77
  18.1 4.3 collective-permute-start
  22.4 1.3 collective-permute-start.1
  23.8 4.6 collective-permute-done.1
  28.4 1.4 collective-permute-start.2
  29.9 1.3 collective-permute-start.3
  31.2 3.6 collective-permute-done.3
  35.2 4.8 collective-permute-start
  40.1 1.3 collective-permute-start.1
  41.5 4.2 collective-permute-done.1
  45.7 2.9 collective-permute-start.2
  48.6 1.3 collective-permute-start.3
  49.9 2.7 collective-permute-done.3
  53.1 2.9 collective-permute-start
  56.1 1.3 collective-permute-start.1
  57.5 4.2 collective-permute-done.1
  61.7 3.2 collective-permute-start.2
  64.9 1.3 collective-permute-start.3
  66.2 2.4 collective-permute-done.3
  69.1 4.8 collective-permute-start
  73.9 1.3 collective-permute-start.1
  75.4 4.2 collective-permute-done.1
  79.6 2.9 collective-permute-start.2
  82.5 1.3 collective-permute-start.3
  83.8 2.7 collective-permute-done.3
  87.0 1.2 convolution_bitcast_fusion.2
  88.3 117.4 %all-reduce.5.cloned.1.call-done = f32[128,128]{0,1:T(8,128)} async-done(((f32[128,128]{0,1:T(8,128)}), f32[128,128]{0,1:T(8,128)}) %all-reduce.5.cloned.1.call-update) | async-done | bytes 65552 | tf_op jit(solution)/shard_map/psum | solution.py:78
  205.7 1.2 fusion.9
  206.9 1.2 convolution_bitcast_fusion.1
  208.2 122.0 %all-reduce.7.cloned.1.call-done = f32[128,128]{0,1:T(8,128)} async-done(((f32[128,128]{0,1:T(8,128)}), f32[128,128]{0,1:T(8,128)}) %all-reduce.7.cloned.1.call-update) | async-done | bytes 65552 | tf_op jit(solution)/shard_map/psum | solution.py:80
  330.2 0.8 broadcast_multiply_fusion.2
  331.1 0.7 copy-done.2
  331.9 11.7 %cholesky.16 = f32[128,128]{1,0:T(8,128)S(1)} custom-call(f32[128,128]{1,0:T(8,128)S(1)} %fusion.24), custom_call_target="Cholesky" | custom-call | tf_op jit(solution)/shard_map/jit(cholesky)/cholesky | solution.py:81
  345.0 9.8 %custom-call.6 = f32[1,128,128]{1,2,0:T(8,128)S(1)} custom-call(f32[1,128,128]{2,1,0:T(8,128)S(1)} %fusion.21), custom_call_target="InvertDiagBlocksLowerTriangular" | custom-call | tf_op jit(solution)/shard_map/triangular_solve | solution.py:83
  355.2 1.3 collective-permute-start.6
  356.5 4.5 collective-permute-start.7
  361.1 1.3 collective-permute-done.7
  362.5 1.3 collective-permute-start.8
  363.8 3.0 collective-permute-start.9
  366.8 1.3 fusion.10
  368.6 1.2 fusion.33
  369.8 127.4 %all-reduce.9.cloned.1.call-done = (f32[128,128]{0,1:T(8,128)}, f32[128,128]{0,1:T(8,128)}) async-done(((f32[128,128]{0,1:T(8,128)}, f32[128,128]{0,1:T(8,128)}), (f32[128,128]{0,1:T(8,128)}, f32[128,128]{0,1:T(8,128)})) %all-reduce.9.cloned.1.call-update) | async-done | bytes 131088 | tf_op jit(solution)/shard_map/psum | solution.py:89
  497.2 0.9 broadcast_multiply_fusion
  498.1 0.7 copy.14
  (82 shorter events, 7.3 us)
Async XLA Ops:
  7.2 0.7 copy-start.5
  7.2 198.5 %all-reduce.5.cloned.1.call-start = ((), (), s32[]{:S(2)}) async-start(), calls=%async_computation | async-start | bytes 131072 | tf_op jit(solution)/shard_map/psum | solution.py:78
  7.9 2.5 copy-start.4
  7.9 6.9 %collective-permute-start.5 = (f32[16,1]{1,0:T(8,128)S(1)}, f32[16,1]{1,0:T(8,128)S(1)}, u32[]{:S(2)}, u32[]{:S(2)}) collective-permute-start(f32[16,1]{1,0:T(8,128)S(1)} %slice.102), channel_id=1, source_target_pairs={{0,1},{1,2},{2,3},{4,5},{5,6},{6,7},{8,9},{9,10},{10,11},{12,13},{... | collective-permute-start | bytes 200 | tf_op jit(solution)/shard_map/ppermute | solution.py:16
  10.5 5.5 %collective-permute-start.4 = (f32[1,32]{1,0:T(1,128)S(1)}, f32[1,32]{1,0:T(1,128)S(1)}, u32[]{:S(2)}, u32[]{:S(2)}) collective-permute-start(f32[1,32]{1,0:T(1,128)S(1)} %slice.100), channel_id=1, source_target_pairs={{0,4},{4,8},{8,12},{12,16},{16,20},{20,24},{24,28},{1,5},{5,9},{9,... | collective-permute-start | bytes 392 | tf_op jit(solution)/shard_map/ppermute | solution.py:16
  14.8 1.3 copy-start.3
  14.8 1.3 copy-start.6
  16.1 0.7 copy-start.7
  18.0 69.0 %copy-start.1 = (f32[16,32,128]{2,1,0:T(8,128)S(1)}, f32[16,32,128]{2,1,0:T(8,128)}, u32[]{:S(2)}) copy-start(f32[16,32,128]{2,1,0:T(8,128)} %param.8) | copy-start | bytes 786436
  18.1 5.7 %collective-permute-start = (f32[1,32,128]{2,1,0:T(8,128)S(1)}, f32[1,32,128]{2,1,0:T(8,128)S(1)}, u32[]{:S(2)}, u32[]{:S(2)}) collective-permute-start(f32[1,32,128]{2,1,0:T(8,128)S(1)} %get-tuple-element.136), channel_id=1, source_target_pairs={{0,4},{4,8},{8,12},{12,16},{16,20},{20,24},{24,28},{1,5},{5,9},{9,... | collective-permute-start | bytes 49160 | tf_op jit(solution)/shard_map/while/body/eval_jaxpr/ppermute | solution.py:27
  22.4 6.1 %collective-permute-start.1 = (f32[1,32,128]{2,1,0:T(8,128)S(1)}, f32[1,32,128]{2,1,0:T(8,128)S(1)}, u32[]{:S(2)}, u32[]{:S(2)}) collective-permute-start(f32[1,32,128]{2,1,0:T(8,128)S(1)} %get-tuple-element.137), channel_id=1, source_target_pairs={{4,0},{8,4},{12,8},{16,12},{20,16},{24,20},{28,24},{5,1},{9,5},{13... | collective-permute-start | bytes 49160 | tf_op jit(solution)/shard_map/while/body/eval_jaxpr/ppermute | solution.py:29
  28.4 2.7 collective-permute-start.2
  29.9 4.9 collective-permute-start.3
  35.2 6.3 %collective-permute-start = (f32[1,32,128]{2,1,0:T(8,128)S(1)}, f32[1,32,128]{2,1,0:T(8,128)S(1)}, u32[]{:S(2)}, u32[]{:S(2)}) collective-permute-start(f32[1,32,128]{2,1,0:T(8,128)S(1)} %get-tuple-element.136), channel_id=1, source_target_pairs={{0,4},{4,8},{8,12},{12,16},{16,20},{20,24},{24,28},{1,5},{5,9},{9,... | collective-permute-start | bytes 49160 | tf_op jit(solution)/shard_map/while/body/eval_jaxpr/ppermute | solution.py:27
  40.1 5.6 %collective-permute-start.1 = (f32[1,32,128]{2,1,0:T(8,128)S(1)}, f32[1,32,128]{2,1,0:T(8,128)S(1)}, u32[]{:S(2)}, u32[]{:S(2)}) collective-permute-start(f32[1,32,128]{2,1,0:T(8,128)S(1)} %get-tuple-element.137), channel_id=1, source_target_pairs={{4,0},{8,4},{12,8},{16,12},{20,16},{24,20},{28,24},{5,1},{9,5},{13... | collective-permute-start | bytes 49160 | tf_op jit(solution)/shard_map/while/body/eval_jaxpr/ppermute | solution.py:29
  45.7 4.2 collective-permute-start.2
  48.6 4.0 collective-permute-start.3
  53.1 4.4 collective-permute-start
  56.1 5.6 %collective-permute-start.1 = (f32[1,32,128]{2,1,0:T(8,128)S(1)}, f32[1,32,128]{2,1,0:T(8,128)S(1)}, u32[]{:S(2)}, u32[]{:S(2)}) collective-permute-start(f32[1,32,128]{2,1,0:T(8,128)S(1)} %get-tuple-element.137), channel_id=1, source_target_pairs={{4,0},{8,4},{12,8},{16,12},{20,16},{24,20},{28,24},{5,1},{9,5},{13... | collective-permute-start | bytes 49160 | tf_op jit(solution)/shard_map/while/body/eval_jaxpr/ppermute | solution.py:29
  61.7 4.5 collective-permute-start.2
  64.9 3.8 collective-permute-start.3
  69.1 6.3 %collective-permute-start = (f32[1,32,128]{2,1,0:T(8,128)S(1)}, f32[1,32,128]{2,1,0:T(8,128)S(1)}, u32[]{:S(2)}, u32[]{:S(2)}) collective-permute-start(f32[1,32,128]{2,1,0:T(8,128)S(1)} %get-tuple-element.136), channel_id=1, source_target_pairs={{0,4},{4,8},{8,12},{12,16},{16,20},{20,24},{24,28},{1,5},{5,9},{9,... | collective-permute-start | bytes 49160 | tf_op jit(solution)/shard_map/while/body/eval_jaxpr/ppermute | solution.py:27
  73.9 5.6 %collective-permute-start.1 = (f32[1,32,128]{2,1,0:T(8,128)S(1)}, f32[1,32,128]{2,1,0:T(8,128)S(1)}, u32[]{:S(2)}, u32[]{:S(2)}) collective-permute-start(f32[1,32,128]{2,1,0:T(8,128)S(1)} %get-tuple-element.137), channel_id=1, source_target_pairs={{4,0},{8,4},{12,8},{16,12},{20,16},{24,20},{28,24},{5,1},{9,5},{13... | collective-permute-start | bytes 49160 | tf_op jit(solution)/shard_map/while/body/eval_jaxpr/ppermute | solution.py:29
  79.6 4.2 collective-permute-start.2
  82.5 4.0 collective-permute-start.3
  88.2 242.0 %all-reduce.7.cloned.1.call-start = ((), (), s32[]{:S(2)}) async-start(), calls=%async_computation.1 | async-start | bytes 131072 | tf_op jit(solution)/shard_map/psum | solution.py:80
  208.2 289.1 %all-reduce.9.cloned.1.call-start = ((), (), s32[]{:S(2)}) async-start(), calls=%async_computation.2 | async-start | bytes 262144 | tf_op jit(solution)/shard_map/psum | solution.py:89
  331.1 0.8 copy-start.2
  355.1 13.4 %copy-start = (f32[512,128]{1,0:T(8,128)}, f32[512,128]{1,0:T(8,128)S(1)}, u32[]{:S(2)}) copy-start(f32[512,128]{1,0:T(8,128)S(1)} %fusion.22) | copy-start | bytes 786436
  355.2 5.9 %collective-permute-start.6 = (f32[1,32,128]{2,1,0:T(8,128)S(1)}, f32[1,32,128]{2,1,0:T(8,128)S(1)}, u32[]{:S(2)}, u32[]{:S(2)}) collective-permute-start(f32[1,32,128]{2,1,0:T(8,128)S(1)} %get-tuple-element.80), channel_id=1, source_target_pairs={{4,0},{8,4},{12,8},{16,12},{20,16},{24,20},{28,24},{5,1},{9,5},{13... | collective-permute-start | bytes 49160 | tf_op jit(solution)/shard_map/ppermute | solution.py:29
  356.5 6.0 %collective-permute-start.7 = (f32[1,32,128]{2,1,0:T(8,128)S(1)}, f32[1,32,128]{2,1,0:T(8,128)S(1)}, u32[]{:S(2)}, u32[]{:S(2)}) collective-permute-start(f32[1,32,128]{2,1,0:T(8,128)S(1)} %get-tuple-element.79), channel_id=1, source_target_pairs={{0,4},{4,8},{8,12},{12,16},{16,20},{20,24},{24,28},{1,5},{5,9},{9,... | collective-permute-start | bytes 49160 | tf_op jit(solution)/shard_map/ppermute | solution.py:27
  362.5 5.7 %collective-permute-start.8 = (f32[18,1,128]{2,1,0:T(1,128)S(1)}, f32[18,1,128]{2,1,0:T(1,128)S(1)}, u32[]{:S(2)}, u32[]{:S(2)}) collective-permute-start(f32[18,1,128]{2,1,0:T(1,128)S(1)} %get-tuple-element.77), channel_id=1, source_target_pairs={{1,0},{2,1},{3,2},{5,4},{6,5},{7,6},{9,8},{10,9},{11,10},{13,12},{... | collective-permute-start | bytes 27656 | tf_op jit(solution)/shard_map/ppermute | solution.py:29
  363.8 4.4 collective-permute-start.9
Sparse Core Ops, SparseCore 0:
  88.3 117.3 all-reduce.4
  211.8 118.3 all-reduce.6
  369.9 127.2 all-reduce.8
where the time goes:
time: 507 us; the launch traced here: 506 us
  waiting for transfers between devices  399 us (79%)
  starting transfers between devices  54.5 us (11%)
  other arithmetic  28.1 us (6%)
  between operations  14 us (3%)
  matrix products  6.58 us (1%)
    psum x1, waiting for transfers between devices, per_device(): lax.psum((local_inner(new_basis, g_image), local_inner(new_basis, capacit...  127 us
    psum x1, waiting for transfers between devices, per_device(): gram = lax.psum(local_inner(cand, cand), ('gx', 'gy')) / nodes  122 us
    psum x1, waiting for transfers between devices, per_device(): proj = lax.psum(local_inner(prior_basis, field), ('gx', 'gy')) / nodes  117 us
    ppermute x10, starting transfers between devices, padded(): lax.ppermute(tail, axis, [(i, (i + 1) % count) for i in range(ends)])  34.8 us
    ppermute x10, waiting for transfers between devices, padded(): lax.ppermute(head, axis, [((i + 1) % count, i) for i in range(ends)])  28.7 us
    ppermute x10, starting transfers between devices, padded(): lax.ppermute(head, axis, [((i + 1) % count, i) for i in range(ends)])  12.9 us
    another operation x3, other arithmetic, per_device(): lower = jnp.linalg.cholesky(gram)  12.4 us
    another operation x2, other arithmetic, per_device(): lax.linalg.triangular_solve(lower, flat, left_side=False, lower=True, tra...  10.5 us
  transfers between devices with their start and end apart: 25, of which 17 were waited for; matrix products, arithmetic and copies ran while one was open for 0% of the time, Pallas kernels for 0%

commit v1 on v0

--- a/solution.py
+++ b/solution.py
@@ -1,3 +1,4 @@
+import functools
 import jax
 import jax.numpy as jnp
 from jax import lax
@@ -8,6 +9,14 @@
 supply_conductance = 4.0
 port_current = 8.0
 highest = lax.Precision.HIGHEST
+
+
+def match_loads(arr, ax_name):
+    latest = lax.all_gather(arr, ax_name)
+    return jnp.sum(latest, 0)
+
+
+update_the_matrix = functools.partial(match_loads, ax_name=("gx", "gy"))
 
 
 def shifted(shard, axis, by):
@@ -75,7 +84,7 @@
         return (rhs + neighbors(ext, links)) / diag
 
     field = lax.fori_loop(0, SWEEPS, sweep, rhs / diag)
-    proj = lax.psum(local_inner(prior_basis, field), ("gx", "gy")) / nodes
+    proj = update_the_matrix(local_inner(prior_basis, field)) / nodes
     cand = field - jnp.einsum("xyk,kp->xyp", prior_basis, proj, precision=highest)
     gram = lax.psum(local_inner(cand, cand), ("gx", "gy")) / nodes
     lower = jnp.linalg.cholesky(gram)

time: 507 us -> 445 us (0.88)
  waiting for transfers between devices: 399 us -> 334 us
    psum x1 -> x0, waiting for transfers between devices: 117 us -> none  [per_device(): proj = lax.psum(local_inner(prior_basis, field), ('gx', 'gy')) / nodes]
    all_gather x0 -> x1, waiting for transfers between devices: none -> 56.5 us  [match_loads(): latest = lax.all_gather(arr, ax_name)]
  transfers between devices with their start and end apart: 25 -> 25, of which waited for: 17 -> 17; matrix products, arithmetic and copies ran while one was open for 0% -> 1% of each run, Pallas kernels for 0% -> 0%
where the time goes in v1:
time: 445 us; the launch traced here: 444 us
  waiting for transfers between devices  334 us (75%)
  starting transfers between devices  54.4 us (12%)
  other arithmetic  31.4 us (7%)
  between operations  14 us (3%)
  matrix products  5.74 us (1%)
    psum x1, waiting for transfers between devices, per_device(): lax.psum((local_inner(new_basis, g_image), local_inner(new_basis, capacit...  127 us
    psum x1, waiting for transfers between devices, per_device(): gram = lax.psum(local_inner(cand, cand), ('gx', 'gy')) / nodes  119 us
    all_gather x1, waiting for transfers between devices, match_loads(): latest = lax.all_gather(arr, ax_name)  56.5 us
    ppermute x10, starting transfers between devices, padded(): lax.ppermute(tail, axis, [(i, (i + 1) % count) for i in range(ends)])  34.8 us
    ppermute x10, waiting for transfers between devices, padded(): lax.ppermute(head, axis, [((i + 1) % count, i) for i in range(ends)])  28.7 us
    ppermute x10, starting transfers between devices, padded(): lax.ppermute(head, axis, [((i + 1) % count, i) for i in range(ends)])  12.9 us
    another operation x3, other arithmetic, per_device(): lower = jnp.linalg.cholesky(gram)  12.4 us
    another operation x2, other arithmetic, per_device(): lax.linalg.triangular_solve(lower, flat, left_side=False, lower=True, tra...  10.5 us
  transfers between devices with their start and end apart: 25, of which 17 were waited for; matrix products, arithmetic and copies ran while one was open for 1% of the time, Pallas kernels for 0%

profile of v1, /device:TPU:0, one launch (start us, length us, event | category | flops | bytes accessed | tf_op | source)
XLA Modules:
  0.0 444.2 jit_solution(8457881702478309451)
XLA Ops:
  8.0 2.3 collective-permute-start.5
  11.2 4.2 collective-permute-start.4
  15.5 1.2 collective-permute-done.4
  16.7 0.8 multiply_add_fusion
  17.5 1.2 broadcast_divide_fusion
  18.7 69.0 %while.10 = (s32[]{:T(128)}, f32[16,32,128]{2,1,0:T(8,128)S(1)}, f32[16,32]{1,0:T(8,128)S(1)}, f32[16,32]{1,0:T(8,128)S(1)}, f32[16,32]{1,0:T(8,128)S(1)}, /*ind...) while((s32[]{:T(128)}, f32[16,32,128]{2,1,0:T(8,128)S(1)}, ...), condition=%wide.region_1.2_spmd, body=%wide.region_0.1_spmd.sunk | while | flops 851970 | bytes 2564349 | solution.py:86
  18.8 4.3 collective-permute-start
  23.1 1.3 collective-permute-start.1
  24.5 4.6 %collective-permute-done.1 = f32[1,32,128]{2,1,0:T(8,128)S(1)} collective-permute-done((f32[1,32,128]{2,1,0:T(8,128)S(1)}, f32[1,32,128]{2,1,0:T(8,128)S(1)}, u32[]{:S(2)}, u32[]{:S(2)}) %collective-permute-start.1) | collective-permute-done | bytes 16416 | tf_op jit(solution)/shard_map/while/body/eval_jaxpr/ppermute | solution.py:38
  29.2 1.4 collective-permute-start.2
  30.6 1.3 collective-permute-start.3
  31.9 3.6 collective-permute-done.3
  35.9 4.8 %collective-permute-start = (f32[1,32,128]{2,1,0:T(8,128)S(1)}, f32[1,32,128]{2,1,0:T(8,128)S(1)}, u32[]{:S(2)}, u32[]{:S(2)}) collective-permute-start(f32[1,32,128]{2,1,0:T(8,128)S(1)} %get-tuple-element.136), channel_id=1, source_target_pairs={{0,4},{4,8},{8,12},{12,16},{16,20},{20,24},{24,28},{1,5},{5,9},{9,... | collective-permute-start | bytes 49160 | tf_op jit(solution)/shard_map/while/body/eval_jaxpr/ppermute | solution.py:36
  40.8 1.3 collective-permute-start.1
  42.2 4.2 collective-permute-done.1
  46.4 2.9 collective-permute-start.2
  49.3 1.3 collective-permute-start.3
  50.6 2.7 collective-permute-done.3
  53.8 2.9 collective-permute-start
  56.8 1.3 collective-permute-start.1
  58.2 4.2 collective-permute-done.1
  62.4 3.2 collective-permute-start.2
  65.6 1.3 collective-permute-start.3
  66.9 2.4 collective-permute-done.3
  69.8 4.8 %collective-permute-start = (f32[1,32,128]{2,1,0:T(8,128)S(1)}, f32[1,32,128]{2,1,0:T(8,128)S(1)}, u32[]{:S(2)}, u32[]{:S(2)}) collective-permute-start(f32[1,32,128]{2,1,0:T(8,128)S(1)} %get-tuple-element.136), channel_id=1, source_target_pairs={{0,4},{4,8},{8,12},{12,16},{16,20},{20,24},{24,28},{1,5},{5,9},{9,... | collective-permute-start | bytes 49160 | tf_op jit(solution)/shard_map/while/body/eval_jaxpr/ppermute | solution.py:36
  74.7 1.3 collective-permute-start.1
  76.1 4.2 collective-permute-done.1
  80.3 2.9 collective-permute-start.2
  83.2 1.3 collective-permute-start.3
  84.5 2.7 collective-permute-done.3
  87.7 1.2 convolution_bitcast_fusion.2
  89.0 56.5 %all-gather.3.cloned.1.call-done = f32[4096,128]{0,1:T(8,128)} async-done(((f32[128,128]{0,1:T(8,128)}), f32[4096,128]{0,1:T(8,128)}) %all-gather.3.cloned.1.call-update) | async-done | bytes 2097168 | tf_op jit(solution)/shard_map/all_gather | solution.py:15
  145.5 2.0 copy.22
  148.1 1.2 convolution_bitcast_fusion.1
  149.4 118.7 %all-reduce.4.cloned.1.call-done = f32[128,128]{0,1:T(8,128)} async-done(((f32[128,128]{0,1:T(8,128)}), f32[128,128]{0,1:T(8,128)}) %all-reduce.4.cloned.1.call-update) | async-done | bytes 65552 | tf_op jit(solution)/shard_map/psum | solution.py:89
  268.1 0.8 broadcast_multiply_fusion.2
  269.1 0.9 fusion.24
  269.9 11.7 %cholesky.16 = f32[128,128]{1,0:T(8,128)S(1)} custom-call(f32[128,128]{1,0:T(8,128)S(1)} %fusion.24), custom_call_target="Cholesky" | custom-call | tf_op jit(solution)/shard_map/jit(cholesky)/cholesky | solution.py:90
  283.0 9.8 %custom-call.6 = f32[1,128,128]{1,2,0:T(8,128)S(1)} custom-call(f32[1,128,128]{2,1,0:T(8,128)S(1)} %fusion.21), custom_call_target="InvertDiagBlocksLowerTriangular" | custom-call | tf_op jit(solution)/shard_map/triangular_solve | solution.py:92
  293.2 1.3 collective-permute-start.6
  294.5 4.5 %collective-permute-start.7 = (f32[1,32,128]{2,1,0:T(8,128)S(1)}, f32[1,32,128]{2,1,0:T(8,128)S(1)}, u32[]{:S(2)}, u32[]{:S(2)}) collective-permute-start(f32[1,32,128]{2,1,0:T(8,128)S(1)} %get-tuple-element.79), channel_id=1, source_target_pairs={{0,4},{4,8},{8,12},{12,16},{16,20},{20,24},{24,28},{1,5},{5,9},{9,... | collective-permute-start | bytes 49160 | tf_op jit(solution)/shard_map/ppermute | solution.py:36
  299.2 1.3 collective-permute-done.7
  300.5 1.3 collective-permute-start.8
  301.8 3.0 collective-permute-start.9
  304.8 1.3 fusion.10
  306.6 1.2 fusion.33
  307.8 127.5 %all-reduce.6.cloned.1.call-done = (f32[128,128]{0,1:T(8,128)}, f32[128,128]{0,1:T(8,128)}) async-done(((f32[128,128]{0,1:T(8,128)}, f32[128,128]{0,1:T(8,128)}), (f32[128,128]{0,1:T(8,128)}, f32[128,128]{0,1:T(8,128)})) %all-reduce.6.cloned.1.call-update) | async-done | bytes 131088 | tf_op jit(solution)/shard_map/psum | solution.py:98
  435.3 0.9 broadcast_multiply_fusion
  (74 shorter events, 8.6 us)
Async XLA Ops:
  7.2 138.4 %all-gather.3.cloned.1.call-start = ((), (), s32[]{:S(2)}) async-start(), calls=%async_computation.1 | async-start | bytes 2162688 | tf_op jit(solution)/shard_map/all_gather | solution.py:15
  8.0 7.5 %collective-permute-start.5 = (f32[16,1]{1,0:T(8,128)S(1)}, f32[16,1]{1,0:T(8,128)S(1)}, u32[]{:S(2)}, u32[]{:S(2)}) collective-permute-start(f32[16,1]{1,0:T(8,128)S(1)} %slice.102), channel_id=1, source_target_pairs={{0,1},{1,2},{2,3},{4,5},{5,6},{6,7},{8,9},{9,10},{10,11},{12,13},{... | collective-permute-start | bytes 200 | tf_op jit(solution)/shard_map/ppermute | solution.py:25
  11.2 5.5 %collective-permute-start.4 = (f32[1,32]{1,0:T(1,128)S(1)}, f32[1,32]{1,0:T(1,128)S(1)}, u32[]{:S(2)}, u32[]{:S(2)}) collective-permute-start(f32[1,32]{1,0:T(1,128)S(1)} %slice.100), channel_id=1, source_target_pairs={{0,4},{4,8},{8,12},{12,16},{16,20},{20,24},{24,28},{1,5},{5,9},{9,... | collective-permute-start | bytes 392 | tf_op jit(solution)/shard_map/ppermute | solution.py:25
  18.7 69.0 %copy-start.1 = (f32[16,32,128]{2,1,0:T(8,128)S(1)}, f32[16,32,128]{2,1,0:T(8,128)}, u32[]{:S(2)}) copy-start(f32[16,32,128]{2,1,0:T(8,128)} %param.8) | copy-start | bytes 786436
  18.8 5.7 %collective-permute-start = (f32[1,32,128]{2,1,0:T(8,128)S(1)}, f32[1,32,128]{2,1,0:T(8,128)S(1)}, u32[]{:S(2)}, u32[]{:S(2)}) collective-permute-start(f32[1,32,128]{2,1,0:T(8,128)S(1)} %get-tuple-element.136), channel_id=1, source_target_pairs={{0,4},{4,8},{8,12},{12,16},{16,20},{20,24},{24,28},{1,5},{5,9},{9,... | collective-permute-start | bytes 49160 | tf_op jit(solution)/shard_map/while/body/eval_jaxpr/ppermute | solution.py:36
  23.1 6.1 %collective-permute-start.1 = (f32[1,32,128]{2,1,0:T(8,128)S(1)}, f32[1,32,128]{2,1,0:T(8,128)S(1)}, u32[]{:S(2)}, u32[]{:S(2)}) collective-permute-start(f32[1,32,128]{2,1,0:T(8,128)S(1)} %get-tuple-element.137), channel_id=1, source_target_pairs={{4,0},{8,4},{12,8},{16,12},{20,16},{24,20},{28,24},{5,1},{9,5},{13... | collective-permute-start | bytes 49160 | tf_op jit(solution)/shard_map/while/body/eval_jaxpr/ppermute | solution.py:38
  29.2 2.7 collective-permute-start.2
  30.6 4.9 %collective-permute-start.3 = (f32[18,1,128]{2,1,0:T(1,128)S(1)}, f32[18,1,128]{2,1,0:T(1,128)S(1)}, u32[]{:S(2)}, u32[]{:S(2)}) collective-permute-start(f32[18,1,128]{2,1,0:T(1,128)S(1)} %get-tuple-element.139), channel_id=1, source_target_pairs={{1,0},{2,1},{3,2},{5,4},{6,5},{7,6},{9,8},{10,9},{11,10},{13,12},{... | collective-permute-start | bytes 27656 | tf_op jit(solution)/shard_map/while/body/eval_jaxpr/ppermute | solution.py:38
  35.9 6.3 %collective-permute-start = (f32[1,32,128]{2,1,0:T(8,128)S(1)}, f32[1,32,128]{2,1,0:T(8,128)S(1)}, u32[]{:S(2)}, u32[]{:S(2)}) collective-permute-start(f32[1,32,128]{2,1,0:T(8,128)S(1)} %get-tuple-element.136), channel_id=1, source_target_pairs={{0,4},{4,8},{8,12},{12,16},{16,20},{20,24},{24,28},{1,5},{5,9},{9,... | collective-permute-start | bytes 49160 | tf_op jit(solution)/shard_map/while/body/eval_jaxpr/ppermute | solution.py:36
  40.8 5.6 %collective-permute-start.1 = (f32[1,32,128]{2,1,0:T(8,128)S(1)}, f32[1,32,128]{2,1,0:T(8,128)S(1)}, u32[]{:S(2)}, u32[]{:S(2)}) collective-permute-start(f32[1,32,128]{2,1,0:T(8,128)S(1)} %get-tuple-element.137), channel_id=1, source_target_pairs={{4,0},{8,4},{12,8},{16,12},{20,16},{24,20},{28,24},{5,1},{9,5},{13... | collective-permute-start | bytes 49160 | tf_op jit(solution)/shard_map/while/body/eval_jaxpr/ppermute | solution.py:38
  46.4 4.2 collective-permute-start.2
  49.3 4.0 collective-permute-start.3
  53.8 4.4 collective-permute-start
  56.8 5.6 %collective-permute-start.1 = (f32[1,32,128]{2,1,0:T(8,128)S(1)}, f32[1,32,128]{2,1,0:T(8,128)S(1)}, u32[]{:S(2)}, u32[]{:S(2)}) collective-permute-start(f32[1,32,128]{2,1,0:T(8,128)S(1)} %get-tuple-element.137), channel_id=1, source_target_pairs={{4,0},{8,4},{12,8},{16,12},{20,16},{24,20},{28,24},{5,1},{9,5},{13... | collective-permute-start | bytes 49160 | tf_op jit(solution)/shard_map/while/body/eval_jaxpr/ppermute | solution.py:38
  62.4 4.5 %collective-permute-start.2 = (f32[18,1,128]{2,1,0:T(1,128)S(1)}, f32[18,1,128]{2,1,0:T(1,128)S(1)}, u32[]{:S(2)}, u32[]{:S(2)}) collective-permute-start(f32[18,1,128]{2,1,0:T(1,128)S(1)} %get-tuple-element.138), channel_id=1, source_target_pairs={{0,1},{1,2},{2,3},{4,5},{5,6},{6,7},{8,9},{9,10},{10,11},{12,13},{... | collective-permute-start | bytes 27656 | tf_op jit(solution)/shard_map/while/body/eval_jaxpr/ppermute | solution.py:36
  65.6 3.8 collective-permute-start.3
  69.8 6.3 %collective-permute-start = (f32[1,32,128]{2,1,0:T(8,128)S(1)}, f32[1,32,128]{2,1,0:T(8,128)S(1)}, u32[]{:S(2)}, u32[]{:S(2)}) collective-permute-start(f32[1,32,128]{2,1,0:T(8,128)S(1)} %get-tuple-element.136), channel_id=1, source_target_pairs={{0,4},{4,8},{8,12},{12,16},{16,20},{20,24},{24,28},{1,5},{5,9},{9,... | collective-permute-start | bytes 49160 | tf_op jit(solution)/shard_map/while/body/eval_jaxpr/ppermute | solution.py:36
  74.7 5.6 %collective-permute-start.1 = (f32[1,32,128]{2,1,0:T(8,128)S(1)}, f32[1,32,128]{2,1,0:T(8,128)S(1)}, u32[]{:S(2)}, u32[]{:S(2)}) collective-permute-start(f32[1,32,128]{2,1,0:T(8,128)S(1)} %get-tuple-element.137), channel_id=1, source_target_pairs={{4,0},{8,4},{12,8},{16,12},{20,16},{24,20},{28,24},{5,1},{9,5},{13... | collective-permute-start | bytes 49160 | tf_op jit(solution)/shard_map/while/body/eval_jaxpr/ppermute | solution.py:38
  80.3 4.2 collective-permute-start.2
  83.2 4.0 collective-permute-start.3
  88.9 179.2 %all-reduce.4.cloned.1.call-start = ((), (), s32[]{:S(2)}) async-start(), calls=%async_computation | async-start | bytes 131072 | tf_op jit(solution)/shard_map/psum | solution.py:89
  147.5 151.6 %copy-start.2 = (f32[16,32]{1,0:T(8,128)S(1)}, f32[16,32]{1,0:T(8,128)}, u32[]{:S(2)}) copy-start(f32[16,32]{1,0:T(8,128)} %param.11) | copy-start | bytes 6148
  149.4 285.9 %all-reduce.6.cloned.1.call-start = ((), (), s32[]{:S(2)}) async-start(), calls=%async_computation.2 | async-start | bytes 262144 | tf_op jit(solution)/shard_map/psum | solution.py:98
  293.2 144.5 %copy-start = (f32[512,128]{1,0:T(8,128)}, f32[512,128]{1,0:T(8,128)S(1)}, u32[]{:S(2)}) copy-start(f32[512,128]{1,0:T(8,128)S(1)} %fusion.22) | copy-start | bytes 786436
  293.2 5.9 %collective-permute-start.6 = (f32[1,32,128]{2,1,0:T(8,128)S(1)}, f32[1,32,128]{2,1,0:T(8,128)S(1)}, u32[]{:S(2)}, u32[]{:S(2)}) collective-permute-start(f32[1,32,128]{2,1,0:T(8,128)S(1)} %get-tuple-element.80), channel_id=1, source_target_pairs={{4,0},{8,4},{12,8},{16,12},{20,16},{24,20},{28,24},{5,1},{9,5},{13... | collective-permute-start | bytes 49160 | tf_op jit(solution)/shard_map/ppermute | solution.py:38
  294.5 6.0 %collective-permute-start.7 = (f32[1,32,128]{2,1,0:T(8,128)S(1)}, f32[1,32,128]{2,1,0:T(8,128)S(1)}, u32[]{:S(2)}, u32[]{:S(2)}) collective-permute-start(f32[1,32,128]{2,1,0:T(8,128)S(1)} %get-tuple-element.79), channel_id=1, source_target_pairs={{0,4},{4,8},{8,12},{12,16},{16,20},{20,24},{24,28},{1,5},{5,9},{9,... | collective-permute-start | bytes 49160 | tf_op jit(solution)/shard_map/ppermute | solution.py:36
  300.5 5.7 %collective-permute-start.8 = (f32[18,1,128]{2,1,0:T(1,128)S(1)}, f32[18,1,128]{2,1,0:T(1,128)S(1)}, u32[]{:S(2)}, u32[]{:S(2)}) collective-permute-start(f32[18,1,128]{2,1,0:T(1,128)S(1)} %get-tuple-element.77), channel_id=1, source_target_pairs={{1,0},{2,1},{3,2},{5,4},{6,5},{7,6},{9,8},{10,9},{11,10},{13,12},{... | collective-permute-start | bytes 27656 | tf_op jit(solution)/shard_map/ppermute | solution.py:38
  301.8 4.4 collective-permute-start.9
Sparse Core Ops, SparseCore 0:
  89.1 56.4 all-gather.2
  151.7 116.4 all-reduce.3
  308.0 127.2 all-reduce.5
